TPU v7x, 256 devices: a whole 4x4x8 slice. The times are simulated.
256 devices in a mesh: dp: 16 (over y, z_hi, core), tensor: 16 (over z_lo, x).
Axes of the slice: x: 4, y: 4, z: 8 (z_hi: 2, z_lo: 4; z = z_hi * 4 + z_lo), core: 2. Of those that a mesh axis runs over, the one named last changes fastest.
Arguments:
- token_ids: int32 [4096], P('dp'), may hold values from 0 to 128255
- attn_heads: bfloat16 [4096, 8192], P('dp', 'tensor'), may hold values from -6 to 6
- out_proj: bfloat16 [8192, 8192], P('tensor'), may hold values from -0.0625 to 0.0625
- residual: bfloat16 [4096, 8192], P(('dp', 'tensor')), may hold values from -6 to 6
- norm_gain: float32 [8192], replicated, may hold values from 0.5 to 1.5
- twist_in: bfloat16 [8192, 8192], P('dp', 'tensor'), may hold values from -0.0625 to 0.0625
- twist_out: float32 [8192], P('tensor'), may hold values from -0.26516503 to 0.26516503
- token_bias: float32 [128256], replicated, may hold values from -4 to 262
- toxicity: int32 [16], P('dp'), may hold values from 1 to 4
- prompt_len: int32 [16], P('dp'), may hold values from 1 to 128
Outputs:
- twist_vals: float32 [4096], P('dp')
- grad_in: float32 [8192, 8192], P('dp', 'tensor')
- grad_out: float32 [8192], P('tensor')
- grad_bias: float32 [128256], P('dp')
All inputs are finite; a program needn't handle non-finite values.
Results may differ from a plain program's by a relative error of at most 0.033.
Values may be sent and summed in bfloat16 or wider, within the bound.
No kernel may reach another device: no remote copies, remote signals or barrier semaphores. Data moves between devices by JAX's collectives and lax.ppermute only.
A program may use at most 128 MiB of HBM per device.

v0:
```python
import jax
import jax.numpy as jnp
from jax import lax
from jax.sharding import Mesh, PartitionSpec as P

SPLITS = 1


def normalize(hidden, norm_gain):
    values = hidden.astype(jnp.float32)
    scaled = lax.rsqrt(jnp.mean(values * values, axis=-1, keepdims=True) + 1e-05)
    return (values * scaled * norm_gain[None, :]).astype(jnp.bfloat16)


def local(
    token_ids,
    attn_heads,
    out_proj,
    residual,
    norm_gain,
    twist_in,
    twist_out,
    token_bias,
    toxicity,
    prompt_len,
):
    seq_len = attn_heads.shape[0]
    width = out_proj.shape[1]
    vocab_size = token_bias.shape[0]
    n_dp = lax.axis_size("dp")
    r = lax.axis_index("dp")
    j = lax.axis_index(("tz", "tx"))
    rows = residual.shape[0]
    twist_full = lax.all_gather(twist_in, "dp", axis=0, tiled=True)
    resid_pad = lax.dynamic_update_slice(
        jnp.zeros((seq_len, width), residual.dtype), residual, (j * rows, 0)
    )
    partial_sum = jnp.dot(attn_heads, out_proj, preferred_element_type=jnp.float32)
    partial_sum = (partial_sum + resid_pad.astype(jnp.float32)).astype(jnp.bfloat16)
    part = lax.psum_scatter(partial_sum, "tx", scatter_dimension=1, tiled=True)
    part = lax.psum(part, "tz")
    hidden = lax.all_gather(part, "tx", axis=1, tiled=True)
    normed = normalize(hidden, norm_gain)
    pre_act = jnp.dot(normed, twist_full, preferred_element_type=jnp.float32)
    active = jax.nn.silu(pre_act)
    partial_psi = jnp.dot(active, twist_out, precision=lax.Precision.HIGHEST)
    lead = (j == 0).astype(jnp.float32)
    own_bias = token_bias[token_ids]
    row = jnp.concatenate(
        [
            partial_psi + lead * own_bias,
            lead * token_ids.astype(jnp.float32),
            lead * prompt_len.astype(jnp.float32),
            lead * toxicity.astype(jnp.float32),
        ]
    )
    slot = (jnp.arange(n_dp) == r).astype(jnp.float32)
    slab = lax.psum(slot[:, None] * row[None, :], ("dp", "tz", "tx"))
    grid = slab[:, :seq_len]
    ids_all = slab[:, seq_len : 2 * seq_len].astype(jnp.int32)
    plen_all = slab[:, 2 * seq_len]
    tox_all = slab[:, 2 * seq_len + 1]
    live = jnp.arange(seq_len, dtype=jnp.float32)[None, :] >= plen_all[:, None]
    levels = tox_all[:, None] * live.astype(jnp.float32)
    highest = jnp.max(jnp.where(live, grid, -1e30), axis=0)
    expo = jnp.where(live, jnp.exp(jnp.where(live, grid - highest[None, :], -80.0)), 0.0)
    totals = jnp.sum(expo, axis=0)
    lab_sum = jnp.sum(levels, axis=0)
    weights_all = (
        expo / jnp.maximum(totals, 1.0)[None, :] - levels / jnp.maximum(lab_sum, 1.0)[None, :]
    ) / seq_len
    twist_vals = lax.dynamic_index_in_dim(grid, r, axis=0, keepdims=False)
    weights = lax.dynamic_index_in_dim(weights_all, r, axis=0, keepdims=False)
    grad_out = lax.psum(jnp.dot(weights, active, precision=lax.Precision.HIGHEST), "dp")
    slice_len = vocab_size // n_dp
    idx = ids_all.reshape(-1) - r * slice_len
    idx = jnp.where((idx >= 0) & (idx < slice_len), idx, slice_len)
    grad_bias = (
        jnp.zeros((slice_len,), jnp.float32).at[idx].add(weights_all.reshape(-1), mode="drop")
    )
    sigma = jax.nn.sigmoid(pre_act)
    d_pre = (
        weights[:, None] * twist_out[None, :] * sigma * (1.0 + pre_act * (1.0 - sigma))
    ).astype(jnp.bfloat16)
    contract = (((0,), (0,)), ((), ()))
    grad_part = lax.dot_general(normed, d_pre, contract, preferred_element_type=jnp.float32).astype(
        jnp.bfloat16
    )
    hcut = grad_part.shape[1] // SPLITS
    grad_in = jnp.concatenate(
        [
            lax.psum_scatter(
                grad_part[:, s * hcut : (s + 1) * hcut], "dp", scatter_dimension=0, tiled=True
            )
            for s in range(SPLITS)
        ],
        axis=1,
    ).astype(jnp.float32)
    return (twist_vals, grad_in, grad_out, grad_bias)


def solution(mesh):
    n_dp, n_tensor = mesh.devices.shape
    n_x = 4
    split = Mesh(mesh.devices.reshape(n_dp, n_tensor // n_x, n_x), ("dp", "tz", "tx"))
    tensor = ("tz", "tx")
    placed = (
        P("dp"),
        P("dp", tensor),
        P(tensor, None),
        P(("dp",) + tensor, None),
        P(),
        P("dp", tensor),
        P(tensor),
        P(),
        P("dp"),
        P("dp"),
    )
    return jax.shard_map(
        local,
        mesh=split,
        in_specs=placed,
        out_specs=(P("dp"), P("dp", tensor), P(tensor), P("dp")),
        check_vma=False,
    )
```

profile of v0, /device:TPU:2, one launch (start us, length us, event | category | flops | bytes accessed | tf_op | source)
XLA Modules:
  0.0 535.5 jit_solution(12805364486706586550)
XLA Ops:
  7.2 0.0 reduce-scatter.3.cloned.1.call-start
  7.2 0.5 broadcast_in_dim.32
  7.7 1.0 constant_dynamic-update-slice_fusion
  8.7 7.9 %fusion = bf16[256,8192]{1,0:T(8,128)(2,1)} fusion(bf16[256,512]{1,0:T(8,128)(2,1)} %param.11, bf16[512,8192]{1,0:T(8,128)(2,1)} %param.12, bf16[256,8192]{1,0:T(8,128)(2,1)S(1)} %constant_dynamic-update-slice_fusion), kind=kOutput, calls=%fused_computation.6 | convolution fusion | flops 2153775104 | bytes 17039360 | tf_op jit(solution)/shard_map/dot_general | solution.py:38
  16.6 0.0 reduce-scatter.3.cloned.1.call-update
  16.6 0.0 all-reduce.2.cloned.1.call-start
  16.6 51.2 %reduce-scatter.3.cloned.1.call-done = bf16[256,2048]{1,0:T(8,128)(2,1)} async-done(((bf16[256,8192]{1,0:T(8,128)(2,1)}), bf16[256,2048]{1,0:T(8,128)(2,1)}) %reduce-scatter.3.cloned.1.call-update) | async-done | bytes 1048592 | tf_op jit(solution)/shard_map/reduce_scatter | solution.py:40
  67.9 0.0 all-gather.3.cloned.1.call-start
  67.9 67.8 %all-reduce.2.cloned.1.call-done = bf16[256,2048]{1,0:T(8,128)(2,1)} async-done(((bf16[256,2048]{1,0:T(8,128)(2,1)}), bf16[256,2048]{1,0:T(8,128)(2,1)}) %all-reduce.2.cloned.1.call-update) | async-done | bytes 1048592 | tf_op jit(solution)/shard_map/psum | solution.py:41
  135.7 0.0 all-gather.5.cloned.1.call-start
  135.7 0.5 all-gather.5.cloned.1.call-update
  136.3 0.0 reduce-scatter.5.cloned.1.call-start
  137.7 1.7 gather_fusion
  139.4 47.0 %all-gather.3.cloned.1.call-done = bf16[256,8192]{1,0:T(8,128)(2,1)} async-done(((bf16[256,2048]{1,0:T(8,128)(2,1)}), bf16[256,8192]{1,0:T(8,128)(2,1)}) %all-gather.3.cloned.1.call-update) | async-done | bytes 4194320 | tf_op jit(solution)/shard_map/all_gather | solution.py:42
  186.4 3.1 fusion.1
  189.6 108.8 %all-gather.5.cloned.1.call-done = bf16[8192,512]{1,0:T(8,128)(2,1)} async-done(((bf16[512,512]{1,0:T(8,128)(2,1)}), bf16[8192,512]{1,0:T(8,128)(2,1)}) %all-gather.5.cloned.1.call-update) | async-done | bytes 8388624 | tf_op jit(solution)/shard_map/all_gather | solution.py:34
  298.4 7.0 %fusion.5 = f32[256,512]{1,0:T(8,128)S(1)} fusion(bf16[8192,512]{1,0:T(8,128)(2,1)} %all-gather.5.cloned.1.call-done, bf16[256,8192]{1,0:T(8,128)(2,1)} %all-gather.3.cloned.1.call-done, f32[8192]{0:T(1024)S(1)} %copy-done.2, f32[256]{0:T(256)S(1)} %add_rsqrt_fusion), kind=kOutput, calls=%fused_computation.10 | convolution fusion | flops 2155872256 | bytes 13140992 | tf_op jit(solution)/shard_map/dot_general | solution.py:44
  305.4 0.6 fusion.13
  306.0 0.1 pad_maximum_fusion
  306.1 0.1 broadcast_multiply_fusion
  306.2 74.1 %psum.22 = f32[16,514]{1,0:T(8,128)S(1)} all-reduce(f32[16,514]{1,0:T(8,128)S(1)} %broadcast_multiply_fusion), channel_id=1, replica_groups=mesh['dp'=16,'tz'=4,'tx'=4] {'dp','tz','tx'}, use_global_device_ids=true, to_apply=%region_3.4 | all-reduce | flops 8224 | bytes 65792 | tf_op jit(solution)/shard_map/psum | solution.py:58
  380.2 0.2 slice_reduce_fusion.1
  380.4 0.1 select_reduce_fusion.1
  380.5 0.1 fusion.21
  380.6 0.1 fusion.16
  380.7 8.1 %convolution_convert_fusion = bf16[8192,512]{1,0:T(8,128)(2,1)} fusion(bf16[256,8192]{1,0:T(8,128)(2,1)} %all-gather.3.cloned.1.call-done, f32[8192]{0:T(1024)S(1)} %copy-done.2, f32[256]{0:T(256)S(1)} %add_rsqrt_fusion, f32[256,512]{1,0:T(8,128)S(1)} %fusion.5, f32[512]{0:T(512)S(1)} %copy-done.3, f32[256]{0:T(256)S(1)} %bitcast.26), kind=kOutput, calls=%fused_computation.2 | convolution fusion | flops 2161377280 | bytes 13144064 | tf_op jit(solution)/shard_map/dot_general | solution.py:86
  388.9 27.9 %scatter_custom_fusion = f32[8016]{0:T(1024)} fusion(s32[4096]{0:T(1024)S(1)} %bitcast.24, f32[4096]{0:T(1024)S(1)} %bitcast.23, f32[]{:T(128)} %constant.15.clone.1), kind=kCustom, calls=%fused_computation.29 | custom fusion | flops 4096 | bytes 32068 | tf_op jit(solution)/shard_map/scatter-add | solution.py:79
  416.8 0.5 fusion.11
  417.3 52.6 %psum.23 = f32[512]{0:T(512)} all-reduce(f32[512]{0:T(512)S(1)} %bitcast.25), channel_id=1, replica_groups=mesh['dp'=16,'tz'=4,'tx'=4] {'dp'}, use_global_device_ids=true, to_apply=%region_8.9 | all-reduce | flops 512 | bytes 4096 | tf_op jit(solution)/shard_map/psum | solution.py:74
  469.9 0.6 constant_dynamic-slice_fusion.1
  470.4 56.4 %reduce-scatter.5.cloned.1.call-done = bf16[512,512]{1,0:T(8,128)(2,1)} async-done(((bf16[8192,512]{1,0:T(8,128)(2,1)}), bf16[512,512]{1,0:T(8,128)(2,1)}) %reduce-scatter.5.cloned.1.call-update) | async-done | bytes 524304 | tf_op jit(solution)/shard_map/reduce_scatter | solution.py:92
  526.8 2.1 convert_element_type.55
  (23 shorter events, 0.2 us)
Async XLA Ops:
  7.2 130.5 %copy-start = (f32[128256]{0:T(1024)S(1)}, f32[128256]{0:T(1024)}, u32[]{:S(2)}) copy-start(f32[128256]{0:T(1024)} %param.17) | copy-start | bytes 1539076
  7.2 60.7 %reduce-scatter.3.cloned.1.call-start = ((), (), s32[]{:S(2)}) async-start(), calls=%async_computation.2 | async-start | bytes 5242880 | tf_op jit(solution)/shard_map/reduce_scatter | solution.py:40
  8.7 129.0 %copy-start.1 = (s32[256]{0:T(256)S(1)}, s32[256]{0:T(256)}, u32[]{:S(2)}) copy-start(s32[256]{0:T(256)} %param.10) | copy-start | bytes 3076
  16.6 281.8 %copy-start.2 = (f32[8192]{0:T(1024)S(1)}, f32[8192]{0:T(1024)}, u32[]{:S(2)}) copy-start(f32[8192]{0:T(1024)} %param.14) | copy-start | bytes 98308
  16.6 119.1 %all-reduce.2.cloned.1.call-start = ((), (), s32[]{:S(2)}) async-start(), calls=%async_computation.3 | async-start | bytes 2097152 | tf_op jit(solution)/shard_map/psum | solution.py:41
  67.9 118.6 %all-gather.3.cloned.1.call-start = ((), (), s32[]{:S(2)}) async-start(), calls=%async_computation.4 | async-start | bytes 5242880 | tf_op jit(solution)/shard_map/all_gather | solution.py:42
  135.7 162.6 %all-gather.5.cloned.1.call-start = ((), (), s32[]{:S(2)}) async-start(), calls=%async_computation.5 | async-start | bytes 8912896 | tf_op jit(solution)/shard_map/all_gather | solution.py:34
  136.3 390.5 %reduce-scatter.5.cloned.1.call-start = ((), (), s32[]{:S(2)}) async-start(), calls=%async_computation.6 | async-start | bytes 8912896 | tf_op jit(solution)/shard_map/reduce_scatter | solution.py:92
  189.6 115.8 %copy-start.3 = (f32[512]{0:T(512)S(1)}, f32[512]{0:T(512)}, u32[]{:S(2)}) copy-start(f32[512]{0:T(512)} %param.16) | copy-start | bytes 6148
Sparse Core Ops, SparseCore 0:
  16.7 51.0 reduce-scatter.2
  70.5 65.1 all-reduce.1
  137.5 48.9 all-gather.2
  189.0 109.3 all-gather.4
  389.0 137.8 reduce-scatter.4
where the time goes:
time: 536 us; the launch traced here: 535 us
  waiting for transfers between devices  332 us (62%)
  blocking collectives  127 us (24%)
  other arithmetic  33.6 us (6%)
  matrix products  24 us (4%)
  between operations  15.3 us (3%)
    all_gather x1, waiting for transfers between devices, local(): twist_full = lax.all_gather(twist_in, 'dp', axis=0, tiled=True)  109 us
    psum x1, blocking collectives, local(): slab = lax.psum(slot[:, None] * row[None, :], ('dp', 'tz', 'tx'))  74.1 us
    psum x1, waiting for transfers between devices, local(): part = lax.psum(part, 'tz')  67.8 us
    reduce_scatter x1, waiting for transfers between devices, local(): lax.psum_scatter(grad_part[:, s * hcut:(s + 1) * hcut], 'dp', scatter_dim...  56.4 us
    psum x1, blocking collectives, local(): lax.psum(jnp.dot(weights, active, precision=lax.Precision.HIGHEST), 'dp')  52.6 us
    reduce_scatter x1, waiting for transfers between devices, local(): part = lax.psum_scatter(partial_sum, 'tx', scatter_dimension=1, tiled=True)  51.2 us
    all_gather x1, waiting for transfers between devices, local(): hidden = lax.all_gather(part, 'tx', axis=1, tiled=True)  47 us
    scatter-add x1, other arithmetic, local(): jnp.zeros((slice_len,), jnp.float32).at[idx]  27.9 us
  transfers between devices with their start and end apart: 5, of which 5 were waited for; matrix products, arithmetic and copies ran while one was open for 6% of the time, Pallas kernels for 0%

commit v1 on v0

--- a/solution.py
+++ b/solution.py
@@ -71,7 +71,9 @@
     ) / seq_len
     twist_vals = lax.dynamic_index_in_dim(grid, r, axis=0, keepdims=False)
     weights = lax.dynamic_index_in_dim(weights_all, r, axis=0, keepdims=False)
-    grad_out = lax.psum(jnp.dot(weights, active, precision=lax.Precision.HIGHEST), "dp")
+    grad_out = jnp.sum(
+        lax.all_gather(jnp.dot(weights, active, precision=lax.Precision.HIGHEST), "dp"), axis=0
+    )
     slice_len = vocab_size // n_dp
     idx = ids_all.reshape(-1) - r * slice_len
     idx = jnp.where((idx >= 0) & (idx < slice_len), idx, slice_len)

time: 536 us -> 533 us (level)
  blocking collectives: 127 us -> 99.8 us
  waiting for transfers between devices: 332 us -> 355 us
    psum x1 -> x0, blocking collectives: 52.6 us -> none  [local(): lax.psum(jnp.dot(weights, active, precision=lax.Precision.HIGHEST), 'dp')]
    all_gather x0 -> x1, blocking collectives: none -> 25.7 us  [local(): lax.all_gather(jnp.dot(weights, active, precision=lax.Precision.HIGHEST),...]
    reduce_scatter x1, waiting for transfers between devices: 56.4 us -> 80 us  [local(): lax.psum_scatter(grad_part[:, s * hcut:(s + 1) * hcut], 'dp', scatter_dim...]
where the time goes in v1:
time: 533 us
  waiting for transfers between devices  355 us (67%)
  blocking collectives  99.8 us (19%)
  other arithmetic  34.2 us (6%)
  matrix products  24 us (5%)
  between operations  15.3 us (3%)
    all_gather x1, waiting for transfers between devices, local(): twist_full = lax.all_gather(twist_in, 'dp', axis=0, tiled=True)  109 us
    reduce_scatter x1, waiting for transfers between devices, local(): lax.psum_scatter(grad_part[:, s * hcut:(s + 1) * hcut], 'dp', scatter_dim...  80 us
    psum x1, blocking collectives, local(): slab = lax.psum(slot[:, None] * row[None, :], ('dp', 'tz', 'tx'))  74.1 us
    psum x1, waiting for transfers between devices, local(): part = lax.psum(part, 'tz')  67.8 us
    reduce_scatter x1, waiting for transfers between devices, local(): part = lax.psum_scatter(partial_sum, 'tx', scatter_dimension=1, tiled=True)  51.2 us
    all_gather x1, waiting for transfers between devices, local(): hidden = lax.all_gather(part, 'tx', axis=1, tiled=True)  47 us
    scatter-add x1, other arithmetic, local(): jnp.zeros((slice_len,), jnp.float32).at[idx]  27.9 us
    all_gather x1, blocking collectives, local(): lax.all_gather(jnp.dot(weights, active, precision=lax.Precision.HIGHEST),...  25.7 us
  transfers between devices with their start and end apart: 5, of which 5 were waited for; matrix products, arithmetic and copies ran while one was open for 6% of the time, Pallas kernels for 0%

profile of v1, /device:TPU:2, one launch (start us, length us, event | category | flops | bytes accessed | tf_op | source)
XLA Modules:
  0.0 532.8 jit_solution(13980497122949808352)
XLA Ops:
  7.2 0.0 reduce-scatter.3.cloned.1.call-start
  7.2 0.5 broadcast_in_dim.32
  7.7 1.0 constant_dynamic-update-slice_fusion
  8.7 7.9 %fusion = bf16[256,8192]{1,0:T(8,128)(2,1)} fusion(bf16[256,512]{1,0:T(8,128)(2,1)} %param.11, bf16[512,8192]{1,0:T(8,128)(2,1)} %param.12, bf16[256,8192]{1,0:T(8,128)(2,1)S(1)} %constant_dynamic-update-slice_fusion), kind=kOutput, calls=%fused_computation.6 | convolution fusion | flops 2153775104 | bytes 17039360 | tf_op jit(solution)/shard_map/dot_general | solution.py:38
  16.6 0.0 all-reduce.2.cloned.1.call-start
  16.6 51.2 %reduce-scatter.3.cloned.1.call-done = bf16[256,2048]{1,0:T(8,128)(2,1)} async-done(((bf16[256,8192]{1,0:T(8,128)(2,1)}), bf16[256,2048]{1,0:T(8,128)(2,1)}) %reduce-scatter.3.cloned.1.call-update) | async-done | bytes 1048592 | tf_op jit(solution)/shard_map/reduce_scatter | solution.py:40
  67.9 0.0 all-gather.5.cloned.1.call-start
  67.9 67.8 %all-reduce.2.cloned.1.call-done = bf16[256,2048]{1,0:T(8,128)(2,1)} async-done(((bf16[256,2048]{1,0:T(8,128)(2,1)}), bf16[256,2048]{1,0:T(8,128)(2,1)}) %all-reduce.2.cloned.1.call-update) | async-done | bytes 1048592 | tf_op jit(solution)/shard_map/psum | solution.py:41
  135.7 0.0 all-gather.7.cloned.1.call-start
  135.7 0.5 all-gather.7.cloned.1.call-update
  136.3 0.0 reduce-scatter.5.cloned.1.call-start
  137.7 1.7 gather_fusion
  139.4 47.0 %all-gather.5.cloned.1.call-done = bf16[256,8192]{1,0:T(8,128)(2,1)} async-done(((bf16[256,2048]{1,0:T(8,128)(2,1)}), bf16[256,8192]{1,0:T(8,128)(2,1)}) %all-gather.5.cloned.1.call-update) | async-done | bytes 4194320 | tf_op jit(solution)/shard_map/all_gather | solution.py:42
  186.4 3.1 fusion.1
  189.6 108.8 %all-gather.7.cloned.1.call-done = bf16[8192,512]{1,0:T(8,128)(2,1)} async-done(((bf16[512,512]{1,0:T(8,128)(2,1)}), bf16[8192,512]{1,0:T(8,128)(2,1)}) %all-gather.7.cloned.1.call-update) | async-done | bytes 8388624 | tf_op jit(solution)/shard_map/all_gather | solution.py:34
  298.4 7.0 %fusion.5 = f32[256,512]{1,0:T(8,128)S(1)} fusion(bf16[8192,512]{1,0:T(8,128)(2,1)} %all-gather.7.cloned.1.call-done, bf16[256,8192]{1,0:T(8,128)(2,1)} %all-gather.5.cloned.1.call-done, f32[8192]{0:T(1024)S(1)} %copy-done.2, f32[256]{0:T(256)S(1)} %add_rsqrt_fusion), kind=kOutput, calls=%fused_computation.10 | convolution fusion | flops 2155872256 | bytes 13140992 | tf_op jit(solution)/shard_map/dot_general | solution.py:44
  305.4 0.6 fusion.12
  306.0 0.1 pad_maximum_fusion
  306.1 0.1 broadcast_multiply_fusion
  306.2 74.1 %psum.15 = f32[16,514]{1,0:T(8,128)S(1)} all-reduce(f32[16,514]{1,0:T(8,128)S(1)} %broadcast_multiply_fusion), channel_id=1, replica_groups=mesh['dp'=16,'tz'=4,'tx'=4] {'dp','tz','tx'}, use_global_device_ids=true, to_apply=%region_3.4 | all-reduce | flops 8224 | bytes 65792 | tf_op jit(solution)/shard_map/psum | solution.py:58
  380.2 0.2 slice_reduce_fusion.1
  380.4 0.1 select_reduce_fusion.1
  380.5 0.1 fusion.20
  380.6 0.1 fusion.15
  380.7 8.1 %convolution_convert_fusion = bf16[8192,512]{1,0:T(8,128)(2,1)} fusion(bf16[256,8192]{1,0:T(8,128)(2,1)} %all-gather.5.cloned.1.call-done, f32[8192]{0:T(1024)S(1)} %copy-done.2, f32[256]{0:T(256)S(1)} %add_rsqrt_fusion, f32[256,512]{1,0:T(8,128)S(1)} %fusion.5, f32[512]{0:T(512)S(1)} %copy-done.3, f32[256]{0:T(256)S(1)} %bitcast.28), kind=kOutput, calls=%fused_computation.2 | convolution fusion | flops 2161377280 | bytes 13144064 | tf_op jit(solution)/shard_map/dot_general | solution.py:88
  388.9 0.5 convolution_bitcast_fusion
  389.4 25.7 %all-gather.1 = f32[16,1,512]{2,1,0:T(1,128)S(1)} all-gather(f32[1,1,512]{2,1,0:T(1,128)S(1)} %convolution_bitcast_fusion), channel_id=2, replica_groups=mesh['dp'=16,'tz'=4,'tx'=4] {'dp'}, dimensions={0}, use_global_device_ids=true | all-gather | bytes 34816 | tf_op jit(solution)/shard_map/all_gather | solution.py:75
  415.1 0.6 reduce_sum.39
  415.7 27.9 %scatter_custom_fusion = f32[8016]{0:T(1024)} fusion(s32[4096]{0:T(1024)S(1)} %bitcast.27, f32[4096]{0:T(1024)S(1)} %bitcast.26, f32[]{:T(128)} %constant.15.clone.1), kind=kCustom, calls=%fused_computation.29 | custom fusion | flops 4096 | bytes 32068 | tf_op jit(solution)/shard_map/scatter-add | solution.py:81
  443.6 0.6 constant_dynamic-slice_fusion.1
  444.2 80.0 %reduce-scatter.5.cloned.1.call-done = bf16[512,512]{1,0:T(8,128)(2,1)} async-done(((bf16[8192,512]{1,0:T(8,128)(2,1)}), bf16[512,512]{1,0:T(8,128)(2,1)}) %reduce-scatter.5.cloned.1.call-update) | async-done | bytes 524304 | tf_op jit(solution)/shard_map/reduce_scatter | solution.py:94
  524.1 2.1 convert_element_type.55
  (24 shorter events, 0.2 us)
Async XLA Ops:
  7.2 130.5 %copy-start = (f32[128256]{0:T(1024)S(1)}, f32[128256]{0:T(1024)}, u32[]{:S(2)}) copy-start(f32[128256]{0:T(1024)} %param.17) | copy-start | bytes 1539076
  7.2 60.7 %reduce-scatter.3.cloned.1.call-start = ((), (), s32[]{:S(2)}) async-start(), calls=%async_computation.2 | async-start | bytes 5242880 | tf_op jit(solution)/shard_map/reduce_scatter | solution.py:40
  8.7 129.0 %copy-start.1 = (s32[256]{0:T(256)S(1)}, s32[256]{0:T(256)}, u32[]{:S(2)}) copy-start(s32[256]{0:T(256)} %param.10) | copy-start | bytes 3076
  16.6 281.8 %copy-start.2 = (f32[8192]{0:T(1024)S(1)}, f32[8192]{0:T(1024)}, u32[]{:S(2)}) copy-start(f32[8192]{0:T(1024)} %param.14) | copy-start | bytes 98308
  16.6 119.1 %all-reduce.2.cloned.1.call-start = ((), (), s32[]{:S(2)}) async-start(), calls=%async_computation.3 | async-start | bytes 2097152 | tf_op jit(solution)/shard_map/psum | solution.py:41
  67.9 118.6 %all-gather.5.cloned.1.call-start = ((), (), s32[]{:S(2)}) async-start(), calls=%async_computation.4 | async-start | bytes 5242880 | tf_op jit(solution)/shard_map/all_gather | solution.py:42
  135.7 162.6 %all-gather.7.cloned.1.call-start = ((), (), s32[]{:S(2)}) async-start(), calls=%async_computation.5 | async-start | bytes 8912896 | tf_op jit(solution)/shard_map/all_gather | solution.py:34
  136.3 387.8 %reduce-scatter.5.cloned.1.call-start = ((), (), s32[]{:S(2)}) async-start(), calls=%async_computation.6 | async-start | bytes 8912896 | tf_op jit(solution)/shard_map/reduce_scatter | solution.py:94
  189.6 115.8 %copy-start.3 = (f32[512]{0:T(512)S(1)}, f32[512]{0:T(512)}, u32[]{:S(2)}) copy-start(f32[512]{0:T(512)} %param.16) | copy-start | bytes 6148
Sparse Core Ops, SparseCore 0:
  16.7 51.0 reduce-scatter.2
  70.5 65.1 all-reduce.1
  137.5 48.9 all-gather.4
  189.0 109.3 all-gather.6
  389.0 135.1 reduce-scatter.4
